TPU v7x, 32 devices: a whole 2x2x4 slice. The times are simulated.
32 devices in a mesh: dp: 4 (over z), expert: 4 (over y, x), tensor: 2 (over core).
Axes of the slice: x: 2, y: 2, z: 4, core: 2. Of those that a mesh axis runs over, the one named last changes fastest.
Arguments:
- tokens: bfloat16 [2048, 2048], P(('dp', 'expert')), may hold values from -6 to 6
- grad_out: bfloat16 [2048, 2048], P(('dp', 'expert')), may hold values from -6 to 6
- route_ids: int32 [2048, 8], P(('dp', 'expert')), may hold values from 0 to 15, all different within a row; in each aligned block of 128 rows (0 to 127, 128 to 255, ...) at most 72 rows name the same one
- gate_values: bfloat16 [2048, 8], P(('dp', 'expert')), may hold values from 0.049804688 to 0.5
- gate_proj: bfloat16 [16, 2048, 768], P(('dp', 'expert'), None, 'tensor'), may hold values from -0.125 to 0.125
- up_proj: bfloat16 [16, 2048, 768], P(('dp', 'expert'), None, 'tensor'), may hold values from -0.125 to 0.125
- down_proj: bfloat16 [16, 768, 2048], P(('dp', 'expert'), 'tensor'), may hold values from -0.21875 to 0.21875
Outputs:
- token_grad: bfloat16 [2048, 2048], P(('dp', 'expert'), 'tensor')
- gate_grad: bfloat16 [2048, 8], P(('dp', 'expert'))
- gate_proj_grad: bfloat16 [16, 2048, 768], P(('dp', 'expert'), None, 'tensor')
- up_proj_grad: bfloat16 [16, 2048, 768], P(('dp', 'expert'), None, 'tensor')
- down_proj_grad: bfloat16 [16, 768, 2048], P(('dp', 'expert'), 'tensor')
Inputs may be any that keep to these rules, and one draw needn't show every extreme that they name: `route_ids`: each token names 8 different experts. Among the rows of one device (128 tokens), no expert is named more than 72 times, a bound that some block reaches.
All inputs are finite; a program needn't handle non-finite values.
Results may differ from a plain program's by a relative error of at most 0.008.
Values may be sent and summed in bfloat16 or wider, within the bound.
No kernel may reach another device: no remote copies, remote signals or barrier semaphores. Data moves between devices by JAX's collectives and lax.ppermute only.
A program may use at most 128 MiB of HBM per device.

v0:
```python
import jax
import jax.numpy as jnp
from jax import lax
from jax.sharding import PartitionSpec as P


def on_device(tokens, grad_out, route_ids, gate_values, gate_proj, up_proj, down_proj):
    tok_rows, features = tokens.shape
    top_count = route_ids.shape[1]
    groups = lax.axis_size(("dp", "expert"))
    capacity = max(2, tok_rows * top_count * 9 // (8 * groups))
    flat_ids = route_ids.reshape(-1)
    expert_iota = jnp.arange(groups, dtype=jnp.int32)
    one_hot = (flat_ids[:, None] == expert_iota[None, :]).astype(jnp.int32)
    position = jnp.sum((jnp.cumsum(one_hot, axis=0) - 1) * one_hot, axis=1)
    slot_index = flat_ids * capacity + position
    entry_of = jnp.full((groups * capacity,), -1, jnp.int32)
    entry_of = entry_of.at[slot_index].set(jnp.arange(tok_rows * top_count, dtype=jnp.int32))
    valid_mask = entry_of >= 0
    safe_entry = jnp.where(valid_mask, entry_of, 0)
    token_index = safe_entry // top_count
    send_x = jnp.where(valid_mask[:, None], tokens[token_index], jnp.zeros((), tokens.dtype))
    send_dy = jnp.where(valid_mask[:, None], grad_out[token_index], jnp.zeros((), grad_out.dtype))
    send_gate = jnp.where(
        valid_mask, gate_values.reshape(-1)[safe_entry], jnp.zeros((), gate_values.dtype)
    )
    routed_x, routed_dy, routed_gate = (
        lax.all_to_all(send_x, ("dp", "expert"), split_axis=0, concat_axis=0, tiled=True),
        lax.all_to_all(send_dy, ("dp", "expert"), split_axis=0, concat_axis=0, tiled=True),
        lax.all_to_all(send_gate, ("dp", "expert"), split_axis=0, concat_axis=0, tiled=True),
    )
    weight_g = gate_proj[0]
    weight_u = up_proj[0]
    weight_d = down_proj[0]
    gate_pre = jnp.dot(routed_x, weight_g, preferred_element_type=jnp.float32)
    up_pre = jnp.dot(routed_x, weight_u, preferred_element_type=jnp.float32)
    sig_gate = jax.nn.sigmoid(gate_pre)
    silu_gate = gate_pre * sig_gate
    activation = (silu_gate * up_pre).astype(jnp.bfloat16)
    hidden_grad = lax.dot_general(
        routed_dy, weight_d, (((1,), (1,)), ((), ())), preferred_element_type=jnp.float32
    )
    gate_terms = jnp.sum(hidden_grad * activation.astype(jnp.float32), axis=1)
    row_gate = routed_gate.astype(jnp.float32)[:, None]
    scaled = row_gate * hidden_grad
    up_grad = (scaled * silu_gate).astype(jnp.bfloat16)
    pre_grad = (scaled * up_pre * sig_gate * (1.0 + gate_pre * (1.0 - sig_gate))).astype(
        jnp.bfloat16
    )
    grad_g = lax.dot_general(
        routed_x, pre_grad, (((0,), (0,)), ((), ())), preferred_element_type=jnp.float32
    ).astype(jnp.bfloat16)
    grad_u = lax.dot_general(
        routed_x, up_grad, (((0,), (0,)), ((), ())), preferred_element_type=jnp.float32
    ).astype(jnp.bfloat16)
    weighted = (row_gate * activation.astype(jnp.float32)).astype(jnp.bfloat16)
    grad_d = lax.dot_general(
        weighted, routed_dy, (((0,), (0,)), ((), ())), preferred_element_type=jnp.float32
    ).astype(jnp.bfloat16)
    partial_value = lax.dot_general(
        pre_grad, weight_g, (((1,), (1,)), ((), ())), preferred_element_type=jnp.float32
    ) + lax.dot_general(
        up_grad, weight_u, (((1,), (1,)), ((), ())), preferred_element_type=jnp.float32
    )
    routed_grad = lax.psum_scatter(partial_value, "tensor", scatter_dimension=1, tiled=True).astype(
        jnp.bfloat16
    )
    slot_gate = lax.psum(gate_terms, "tensor").astype(jnp.bfloat16)
    back_rows, back_gate = (
        lax.all_to_all(routed_grad, ("dp", "expert"), split_axis=0, concat_axis=0, tiled=True),
        lax.all_to_all(slot_gate, ("dp", "expert"), split_axis=0, concat_axis=0, tiled=True),
    )
    picked = (
        back_rows[slot_index].astype(jnp.float32).reshape(tok_rows, top_count, back_rows.shape[1])
    )
    token_grad = jnp.sum(picked, axis=1).astype(jnp.bfloat16)
    gate_grad = back_gate[slot_index].reshape(tok_rows, top_count)
    return (token_grad, gate_grad, grad_g[None], grad_u[None], grad_d[None])


def solution(mesh):
    in_specs = (
        P(("dp", "expert"), None),
        P(("dp", "expert"), None),
        P(("dp", "expert"), None),
        P(("dp", "expert"), None),
        P(("dp", "expert"), None, "tensor"),
        P(("dp", "expert"), None, "tensor"),
        P(("dp", "expert"), "tensor", None),
    )
    out_specs = (
        P(("dp", "expert"), "tensor"),
        P(("dp", "expert"), None),
        P(("dp", "expert"), None, "tensor"),
        P(("dp", "expert"), None, "tensor"),
        P(("dp", "expert"), "tensor", None),
    )
    return jax.shard_map(
        on_device, mesh=mesh, in_specs=in_specs, out_specs=out_specs, check_vma=False
    )
```

profile of v0, /device:TPU:0, one launch (start us, length us, event | category | flops | bytes accessed | tf_op | source)
XLA Modules:
  0.0 386.3 jit_solution(4429680165145374496)
XLA Ops:
  7.2 0.0 copy-start
  7.2 0.8 broadcast_multiply_fusion
  8.0 0.8 copy.22
  8.8 0.1 eq.29
  8.9 0.1 eq.25
  9.0 0.8 copy.26
  9.8 0.1 reshape.96
  9.9 0.1 copy.21
  10.0 0.1 mul.59
  10.1 4.5 %reduce-window.6 = s32[16,8,128]{2,1,0:T(8,128)S(1)} reduce-window(s32[16,8,128]{2,1,0:T(8,128)S(1)} %fusion.19, s32[]{:T(128)} %constant.16.clone.1), window={size=1x1x128 pad=0_0x0_0x127_0}, to_apply=%region_0.0 | reduce-window | flops 2080768 | bytes 131076 | tf_op jit(solution)/shard_map/reduce-window
  14.6 0.1 slice.18
  14.7 0.1 copy.24
  14.8 0.1 copy.25
  14.9 0.1 add_add_fusion
  15.1 4.3 %scatter_custom_fusion = s32[1152]{0:T(1024)S(1)} fusion(s32[1024]{0:T(1024)S(1)} %bitcast.70, s32[1024]{0:T(1024)S(1)} %iota.11, s32[]{:T(128)} %constant.13.clone.1), kind=kCustom, calls=%fused_computation.56 | custom fusion | bytes 4612 | tf_op jit(solution)/shard_map/scatter | solution.py:18
  19.4 0.0 copy-start.2
  19.4 7.3 %gather_fusion = bf16[1152]{0:T(1024)(128)(2,1)S(1)} fusion(bf16[1024]{0:T(1024)(128)(2,1)S(1)} %reshape.96, s32[2048]{0:T(1024)S(1)} %pad_clamp_fusion.1), kind=kCustom, calls=%fused_computation | custom fusion | bytes 9216 | tf_op jit(solution)/shard_map/gather | solution.py:25
  26.7 0.7 all_to_all.46
  27.4 8.3 %all-to-all-start = ((bf16[16,72,1]{1,2,0:T(2,128)(2,1)}), bf16[16,72,1]{1,2,0:T(2,128)(2,1)S(1)}, u32[]{:S(2)}, u32[]{:S(2)}) async-start(bf16[16,72,1]{1,2,0:T(2,128)(2,1)} %all_to_all.46), calls=%async_computation | async-start | bytes 16384 | tf_op jit(solution)/shard_map/all_to_all | solution.py:30
  35.8 0.1 broadcast_in_dim.53
  35.9 0.0 copy-done.2
  35.9 0.0 copy-start.3
  35.9 5.9 %gather_fusion.2 = bf16[1152,2048]{1,0:T(8,128)(2,1)} fusion(bf16[128,2048]{1,0:T(8,128)(2,1)S(1)} %copy-done.2, s32[2048]{0:T(1024)S(1)} %pad_clamp_fusion), kind=kCustom, calls=%fused_computation.2 | custom fusion | bytes 9441792 | tf_op jit(solution)/shard_map/gather | solution.py:22
  41.8 0.0 copy-done.3
  41.8 5.9 %gather_fusion.1 = bf16[1152,2048]{1,0:T(8,128)(2,1)} fusion(bf16[128,2048]{1,0:T(8,128)(2,1)S(1)} %copy-done.3, s32[2048]{0:T(1024)S(1)} %pad_clamp_fusion), kind=kCustom, calls=%fused_computation.1 | custom fusion | bytes 9441792 | tf_op jit(solution)/shard_map/gather | solution.py:23
  47.7 8.4 %broadcast_select_fusion.1 = (bf16[16,72,2048]{2,1,0:T(8,128)(2,1)}, bf16[16,72,2048]{2,1,0:T(8,128)(2,1)}) fusion(bf16[16,72,2048]{2,1,0:T(8,128)(2,1)} %bitcast.57, pred[16,72]{1,0:T(8,128)(4,1)S(1)} %broadcast_in_dim.53, bf16[16,72,2048]{2,1,0:T(8,128)(2,1)} %bitcast.56), kind=kLoop, calls=%fused_computation.8 | loop fusion | flops 4718592 | bytes 18875520 | tf_op jit(solution)/shard_map/jit(_where)/select_n | solution.py:23
  56.1 0.0 all-to-all-done
  56.1 111.7 %all_to_all.53 = bf16[16,72,2048]{2,1,0:T(8,128)(2,1)} all-to-all(bf16[16,72,2048]{2,1,0:T(8,128)(2,1)} %get-tuple-element.22), channel_id=1, replica_groups=mesh['dp'=4,'expert'=4,'tensor'=2] {'dp','expert'}, dimensions={0} | all-to-all | bytes 9437184 | tf_op jit(solution)/shard_map/all_to_all | solution.py:28
  167.7 4.7 %all-to-all-start.1 = ((bf16[16,72,2048]{2,1,0:T(8,128)(2,1)}), bf16[16,72,2048]{2,1,0:T(8,128)(2,1)}, u32[]{:S(2)}, u32[]{:S(2)}) async-start(bf16[16,72,2048]{2,1,0:T(8,128)(2,1)} %get-tuple-element.21), calls=%async_computation.1 | async-start | bytes 9437184 | tf_op jit(solution)/shard_map/all_to_all | solution.py:29
  172.4 0.2 reduce-scatter.2.cloned.1.call-start
  172.7 0.1 reshape.98
  172.8 0.0 copy-done
  172.8 0.0 slice-start.1
  172.8 0.0 copy-start.4
  172.8 6.0 %fusion.8 = f32[1152,384]{0,1:T(8,128)} fusion(bf16[1152,2048]{1,0:T(8,128)(2,1)} %bitcast.59, bf16[1,2048,384]{2,1,0:T(8,128)(2,1)S(1)} %copy-done), kind=kOutput, calls=%fused_computation.27 | convolution fusion | flops 1811939328 | bytes 8060928 | tf_op jit(solution)/shard_map/dot_general | solution.py:35
  178.8 0.0 slice-done
  178.8 0.0 slice-done.1
  178.8 0.0 copy-done.4
  178.8 3.5 fusion.11
  182.4 77.4 %all-to-all-done.1 = bf16[16,72,2048]{2,1,0:T(8,128)(2,1)} async-done(((bf16[16,72,2048]{2,1,0:T(8,128)(2,1)}), bf16[16,72,2048]{2,1,0:T(8,128)(2,1)}, u32[]{:S(2)}, u32[]{:S(2)}) %all-to-all-start.1) | async-done | bytes 4718624 | tf_op jit(solution)/shard_map/all_to_all | solution.py:29
  259.7 7.6 %fusion.3 = (f32[1152]{0:T(1024)S(1)}, bf16[1152,384]{0,1:T(8,128)(2,1)}, bf16[1152,384]{0,1:T(8,128)(2,1)S(1)}, bf16[1152,384]{0,1:T(8,128)(2,1)S(1)}) fusion(f32[1152,384]{0,1:T(8,128)} %fusion.11, f32[1152,384]{0,1:T(8,128)} %fusion.8, f32[1152]{0:T(1024)S(1)} %reshape.98, bf16[1152,2048]{1,0:T(8,128)(2,1)} %bitcast.5, bf16[1,384,2048]{2,1,0:T(8,128)(2,1)} %param.13), kind=kOutput, calls=%fused_computation.18 | convolution fusion | flops 1820343168 | bytes 12493824 | tf_op jit(solution)/shard_map/dot_general | solution.py:40
  267.3 2.7 fusion.6
  270.0 5.2 %convolution_add_fusion = f32[1152,2048]{1,0:T(8,128)} fusion(f32[1152,2048]{1,0:T(8,128)S(1)} %fusion.6, bf16[1152,384]{0,1:T(8,128)(2,1)S(1)} %get-tuple-element.20, bf16[1,2048,384]{2,1,0:T(8,128)(2,1)S(1)} %copy-done.5), kind=kOutput, calls=%fused_computation.6 | convolution fusion | flops 1814298624 | bytes 21331968 | tf_op jit(solution)/shard_map/dot_general | solution.py:62
  275.2 0.0 reduce-scatter.2.cloned.1.call-update
  275.3 2.5 psum.7
  277.8 0.7 all_to_all.47
  278.5 21.2 %all-to-all-start.4 = ((bf16[16,72,1]{1,2,0:T(2,128)(2,1)}), bf16[16,72,1]{1,2,0:T(2,128)(2,1)S(1)}, u32[]{:S(2)}, u32[]{:S(2)}) async-start(bf16[16,72,1]{1,2,0:T(2,128)(2,1)} %all_to_all.47), calls=%async_computation.5 | async-start | bytes 16384 | tf_op jit(solution)/shard_map/all_to_all | solution.py:71
  299.7 9.1 %reduce-scatter.2.cloned.1.call-done = f32[1152,1024]{1,0:T(8,128)} async-done(((f32[1152,2048]{1,0:T(8,128)}), f32[1152,1024]{1,0:T(8,128)}) %reduce-scatter.2.cloned.1.call-update) | async-done | bytes 4718608 | tf_op jit(solution)/shard_map/reduce_scatter | solution.py:65
  308.8 4.1 %convert_element_type.54 = bf16[1152,1024]{1,0:T(8,128)(2,1)} convert(f32[1152,1024]{1,0:T(8,128)} %reduce-scatter.2.cloned.1.call-done) | non-fusion elementwise | flops 1179648 | bytes 7077888 | tf_op jit(solution)/shard_map/convert_element_type | solution.py:65
  312.9 0.0 all-to-all-done.4
  312.9 7.0 %all-to-all-start.3 = ((bf16[16,72,1024]{2,1,0:T(8,128)(2,1)}), bf16[16,72,1024]{2,1,0:T(8,128)(2,1)}, u32[]{:S(2)}, u32[]{:S(2)}) async-start(bf16[16,72,1024]{2,1,0:T(8,128)(2,1)} %bitcast.58), calls=%async_computation.4 | async-start | bytes 4718592 | tf_op jit(solution)/shard_map/all_to_all | solution.py:70
  320.0 0.0 slice-start.3
  320.0 6.4 %fusion = bf16[1,2048,384]{2,1,0:T(8,128)(2,1)} fusion(bf16[1152,2048]{1,0:T(8,128)(2,1)} %bitcast.60, bf16[1152,384]{0,1:T(8,128)(2,1)S(1)} %copy-done.7), kind=kOutput, calls=%fused_computation.12 | convolution fusion | flops 1812725760 | bytes 7176192 | tf_op jit(solution)/shard_map/dot_general | solution.py:50
  326.4 0.0 slice-done.2
  326.4 3.9 %fusion.1 = bf16[1,2048,384]{2,1,0:T(8,128)(2,1)} fusion(bf16[1152,2048]{1,0:T(8,128)(2,1)S(1)} %bitcast.66, bf16[1152,384]{0,1:T(8,128)(2,1)S(1)} %get-tuple-element.20), kind=kOutput, calls=%fused_computation.13 | convolution fusion | flops 1812725760 | bytes 7176192 | tf_op jit(solution)/shard_map/dot_general | solution.py:53
  330.4 0.0 copy-done.8
  330.4 5.7 %fusion.2 = bf16[1,384,2048]{2,1,0:T(8,128)(2,1)} fusion(bf16[1152,2048]{1,0:T(8,128)(2,1)} %bitcast.5, bf16[1152,384]{0,1:T(8,128)(2,1)S(1)} %copy-done.8, f32[1152]{0:T(1024)S(1)} %reshape.98), kind=kOutput, calls=%fused_computation.14 | convolution fusion | flops 1814052864 | bytes 7180800 | tf_op jit(solution)/shard_map/dot_general | solution.py:57
  336.1 0.1 all_to_all.45
  336.2 6.8 %gather_fusion.4 = bf16[1024]{0:T(1024)(128)(2,1)S(1)} fusion(bf16[1152]{0:T(1024)(128)(2,1)S(1)} %all_to_all.45, s32[1024]{0:T(1024)S(1)} %broadcast_clamp_fusion), kind=kCustom, calls=%fused_computation.4 | custom fusion | bytes 8192 | tf_op jit(solution)/shard_map/gather | solution.py:77
  343.0 0.1 reshape.97
  343.1 0.7 copy.29
  343.7 23.9 %all-to-all-done.3 = bf16[16,72,1024]{2,1,0:T(8,128)(2,1)} async-done(((bf16[16,72,1024]{2,1,0:T(8,128)(2,1)}), bf16[16,72,1024]{2,1,0:T(8,128)(2,1)}, u32[]{:S(2)}, u32[]{:S(2)}) %all-to-all-start.3) | async-done | bytes 2359328 | tf_op jit(solution)/shard_map/all_to_all | solution.py:70
  367.6 8.1 %gather_fusion.3 = bf16[1024,1024]{1,0:T(8,128)(2,1)} fusion(bf16[1152,1024]{1,0:T(8,128)(2,1)} %bitcast.12, s32[1024]{0:T(1024)S(1)} %broadcast_clamp_fusion), kind=kCustom, calls=%fused_computation.3 | custom fusion | bytes 4198400 | tf_op jit(solution)/shard_map/gather | solution.py:74
  375.7 3.7 bitcast_reduce_fusion
  (28 shorter events, 0.2 us)
Async XLA Ops:
  7.2 165.6 %copy-start = (bf16[1,2048,384]{2,1,0:T(8,128)(2,1)S(1)}, bf16[1,2048,384]{2,1,0:T(8,128)(2,1)}, u32[]{:S(2)}) copy-start(bf16[1,2048,384]{2,1,0:T(8,128)(2,1)} %param.11) | copy-start | bytes 4718596
  19.4 16.5 %copy-start.2 = (bf16[128,2048]{1,0:T(8,128)(2,1)S(1)}, bf16[128,2048]{1,0:T(8,128)(2,1)}, u32[]{:S(2)}) copy-start(bf16[128,2048]{1,0:T(8,128)(2,1)} %param.7) | copy-start | bytes 1572868
  27.4 28.7 %all-to-all-start = ((bf16[16,72,1]{1,2,0:T(2,128)(2,1)}), bf16[16,72,1]{1,2,0:T(2,128)(2,1)S(1)}, u32[]{:S(2)}, u32[]{:S(2)}) async-start(bf16[16,72,1]{1,2,0:T(2,128)(2,1)} %all_to_all.46), calls=%async_computation | async-start | bytes 16384 | tf_op jit(solution)/shard_map/all_to_all | solution.py:30
  35.9 5.9 %copy-start.3 = (bf16[128,2048]{1,0:T(8,128)(2,1)S(1)}, bf16[128,2048]{1,0:T(8,128)(2,1)}, u32[]{:S(2)}) copy-start(bf16[128,2048]{1,0:T(8,128)(2,1)} %param.8) | copy-start | bytes 1572868
  167.7 11.1 %slice-start = ((s8[4718592]{0:T(1024)(128)(4,1)}), s8[524288]{0:T(1024)(128)(4,1)S(1)}, s32[]{:S(2)}) async-start(s8[4718592]{0:T(1024)(128)(4,1)} %bitcast.61), calls=%async_computation.7 | async-start | bytes 1048576
  167.7 92.0 %all-to-all-start.1 = ((bf16[16,72,2048]{2,1,0:T(8,128)(2,1)}), bf16[16,72,2048]{2,1,0:T(8,128)(2,1)}, u32[]{:S(2)}, u32[]{:S(2)}) async-start(bf16[16,72,2048]{2,1,0:T(8,128)(2,1)} %get-tuple-element.21), calls=%async_computation.1 | async-start | bytes 9437184 | tf_op jit(solution)/shard_map/all_to_all | solution.py:29
  172.4 136.3 %reduce-scatter.2.cloned.1.call-start = ((), (), s32[]{:S(2)}) async-start(), calls=%async_computation.6 | async-start | bytes 14155776 | tf_op jit(solution)/shard_map/reduce_scatter | solution.py:65
  172.8 6.0 %slice-start.1 = ((s8[4718592]{0:T(1024)(128)(4,1)}), s8[4194304]{0:T(1024)(128)(4,1)S(1)}, s32[]{:S(2)}) async-start(s8[4718592]{0:T(1024)(128)(4,1)} %bitcast.61), calls=%async_computation.8 | async-start | bytes 8388608
  172.8 6.0 %copy-start.4 = (bf16[1,2048,384]{2,1,0:T(8,128)(2,1)S(1)}, bf16[1,2048,384]{2,1,0:T(8,128)(2,1)}, u32[]{:S(2)}) copy-start(bf16[1,2048,384]{2,1,0:T(8,128)(2,1)} %param.12) | copy-start | bytes 4718596
  267.3 2.7 copy-start.6
  267.3 2.7 copy-start.5
  278.5 34.4 %all-to-all-start.4 = ((bf16[16,72,1]{1,2,0:T(2,128)(2,1)}), bf16[16,72,1]{1,2,0:T(2,128)(2,1)S(1)}, u32[]{:S(2)}, u32[]{:S(2)}) async-start(bf16[16,72,1]{1,2,0:T(2,128)(2,1)} %all_to_all.47), calls=%async_computation.5 | async-start | bytes 16384 | tf_op jit(solution)/shard_map/all_to_all | solution.py:71
  312.9 7.0 %copy-start.7 = (bf16[1152,384]{0,1:T(8,128)(2,1)S(1)}, bf16[1152,384]{0,1:T(8,128)(2,1)}, u32[]{:S(2)}) copy-start(bf16[1152,384]{0,1:T(8,128)(2,1)} %copy-done.6) | copy-start | bytes 2654212
  312.9 13.5 %slice-start.2 = ((s8[4718592]{0:T(1024)(128)(4,1)}), s8[524288]{0:T(1024)(128)(4,1)S(1)}, s32[]{:S(2)}) async-start(s8[4718592]{0:T(1024)(128)(4,1)} %bitcast.64), calls=%async_computation.9 | async-start | bytes 1048576
  312.9 54.7 %all-to-all-start.3 = ((bf16[16,72,1024]{2,1,0:T(8,128)(2,1)}), bf16[16,72,1024]{2,1,0:T(8,128)(2,1)}, u32[]{:S(2)}, u32[]{:S(2)}) async-start(bf16[16,72,1024]{2,1,0:T(8,128)(2,1)} %bitcast.58), calls=%async_computation.4 | async-start | bytes 4718592 | tf_op jit(solution)/shard_map/all_to_all | solution.py:70
  320.0 6.5 %slice-start.3 = ((s8[4718592]{0:T(1024)(128)(4,1)}), s8[4194304]{0:T(1024)(128)(4,1)S(1)}, s32[]{:S(2)}) async-start(s8[4718592]{0:T(1024)(128)(4,1)} %bitcast.64), calls=%async_computation.10 | async-start | bytes 8388608
  326.4 4.0 %copy-start.8 = (bf16[1152,384]{0,1:T(8,128)(2,1)S(1)}, bf16[1152,384]{0,1:T(8,128)(2,1)}, u32[]{:S(2)}) copy-start(bf16[1152,384]{0,1:T(8,128)(2,1)} %get-tuple-element.16) | copy-start | bytes 2654212
  367.6 11.9 %copy-start.1 = (bf16[1,2048,384]{2,1,0:T(8,128)(2,1)S(1)}, bf16[1,2048,384]{2,1,0:T(8,128)(2,1)}, u32[]{:S(2)}) copy-start(bf16[1,2048,384]{2,1,0:T(8,128)(2,1)} %param.11) | copy-start | bytes 4718596
Sparse Core Ops, SparseCore 0:
  275.4 33.3 reduce-scatter.1
where the time goes:
time: 392 us; the launch traced here: 386 us
  blocking collectives  114 us (29%)
  waiting for transfers between devices  110 us (28%)
  local copies, waits for them, and re-layouts  43.2 us (11%)
  starting transfers between devices  41.4 us (11%)
  matrix products  41 us (10%)
  other arithmetic  21.8 us (6%)
  between operations  14.3 us (4%)
    all_to_all x1, blocking collectives, on_device(): lax.all_to_all(send_x, ('dp', 'expert'), split_axis=0, concat_axis=0, til...  112 us
    all_to_all x1, waiting for transfers between devices, on_device(): lax.all_to_all(send_dy, ('dp', 'expert'), split_axis=0, concat_axis=0, ti...  77.4 us
    all_to_all x1, waiting for transfers between devices, on_device(): lax.all_to_all(routed_grad, ('dp', 'expert'), split_axis=0, concat_axis=0...  23.9 us
    all_to_all x1, starting transfers between devices, on_device(): lax.all_to_all(slot_gate, ('dp', 'expert'), split_axis=0, concat_axis=0,...  21.2 us
    reduce_scatter x1, waiting for transfers between devices, on_device(): lax.psum_scatter(partial_value, 'tensor', scatter_dimension=1, tiled=True)  9.1 us
    select_n x1, other arithmetic, on_device(): jnp.where(valid_mask[:, None], grad_out[token_index], jnp.zeros((), grad_...  8.37 us
    all_to_all x1, starting transfers between devices, on_device(): lax.all_to_all(send_gate, ('dp', 'expert'), split_axis=0, concat_axis=0,...  8.31 us
    gather x1, local copies, waits for them, and re-layouts, on_device(): back_rows[slot_index].astype(jnp.float32)  8.12 us
  transfers between devices with their start and end apart: 5, of which 3 were waited for; matrix products, arithmetic and copies ran while one was open for 15% of the time, Pallas kernels for 0%

commit v1 on v0

--- a/solution.py
+++ b/solution.py
@@ -7,28 +7,52 @@
 def on_device(tokens, grad_out, route_ids, gate_values, gate_proj, up_proj, down_proj):
     tok_rows, features = tokens.shape
     top_count = route_ids.shape[1]
-    groups = lax.axis_size(("dp", "expert"))
+    n_dp = lax.axis_size("dp")
+    n_ex = lax.axis_size("expert")
+    groups = n_dp * n_ex
     capacity = max(2, tok_rows * top_count * 9 // (8 * groups))
-    flat_ids = route_ids.reshape(-1)
-    expert_iota = jnp.arange(groups, dtype=jnp.int32)
-    one_hot = (flat_ids[:, None] == expert_iota[None, :]).astype(jnp.int32)
-    position = jnp.sum((jnp.cumsum(one_hot, axis=0) - 1) * one_hot, axis=1)
-    slot_index = flat_ids * capacity + position
-    entry_of = jnp.full((groups * capacity,), -1, jnp.int32)
-    entry_of = entry_of.at[slot_index].set(jnp.arange(tok_rows * top_count, dtype=jnp.int32))
-    valid_mask = entry_of >= 0
-    safe_entry = jnp.where(valid_mask, entry_of, 0)
-    token_index = safe_entry // top_count
-    send_x = jnp.where(valid_mask[:, None], tokens[token_index], jnp.zeros((), tokens.dtype))
-    send_dy = jnp.where(valid_mask[:, None], grad_out[token_index], jnp.zeros((), grad_out.dtype))
-    send_gate = jnp.where(
-        valid_mask, gate_values.reshape(-1)[safe_entry], jnp.zeros((), gate_values.dtype)
+    plane = lax.axis_index("dp")
+    core = lax.axis_index("tensor")
+    col_rows = n_dp * tok_rows
+    plane_slots = n_dp * capacity
+    slots = n_ex * plane_slots
+
+    ids_all = lax.all_gather(route_ids, "dp", tiled=True)
+    gates_all = lax.all_gather(gate_values, "dp", tiled=True)
+
+    carried = jnp.where(core == 0, tokens, grad_out)
+    carried_all = lax.all_gather(carried, "dp", tiled=True)
+
+    routes = tok_rows * top_count
+    ids_blk = ids_all.reshape(n_dp, routes)
+    local_ex = ids_blk - plane * n_ex
+    in_plane = (local_ex >= 0) & (local_ex < n_ex)
+    one_hot = (local_ex[:, :, None] == jnp.arange(n_ex, dtype=jnp.int32)[None, None, :])
+    one_hot_b = one_hot.astype(jnp.bfloat16)
+    r_iota = jnp.arange(routes, dtype=jnp.int32)
+    earlier = (r_iota[None, :] < r_iota[:, None]).astype(jnp.bfloat16)
+    running = jnp.einsum(
+        "ab,nbe->nae", earlier, one_hot_b, preferred_element_type=jnp.float32
     )
-    routed_x, routed_dy, routed_gate = (
-        lax.all_to_all(send_x, ("dp", "expert"), split_axis=0, concat_axis=0, tiled=True),
-        lax.all_to_all(send_dy, ("dp", "expert"), split_axis=0, concat_axis=0, tiled=True),
-        lax.all_to_all(send_gate, ("dp", "expert"), split_axis=0, concat_axis=0, tiled=True),
-    )
+    position = jnp.sum(running * one_hot.astype(jnp.float32), axis=2).astype(jnp.int32)
+    blk = jnp.arange(n_dp, dtype=jnp.int32)[:, None]
+    slot_of = jnp.where(in_plane, local_ex * plane_slots + blk * capacity + position, -1)
+    slot_of = slot_of.reshape(col_rows, top_count)
+
+    s_iota = jnp.arange(slots, dtype=jnp.int32)
+    match = slot_of[None, :, :] == s_iota[:, None, None]
+    select = jnp.sum(match.astype(jnp.bfloat16), axis=2)
+    send = jnp.dot(select, carried_all, preferred_element_type=jnp.float32).astype(tokens.dtype)
+    send_gate = jnp.sum(
+        jnp.where(match, gates_all.astype(jnp.float32)[None, :, :], 0.0), axis=(1, 2)
+    ).astype(gate_values.dtype)
+
+    recv = lax.all_to_all(send, "expert", split_axis=0, concat_axis=0, tiled=True)
+    routed_gate = lax.all_to_all(send_gate, "expert", split_axis=0, concat_axis=0, tiled=True)
+    both = lax.all_gather(recv, "tensor")
+    routed_x = both[0]
+    routed_dy = both[1]
+
     weight_g = gate_proj[0]
     weight_u = up_proj[0]
     weight_d = down_proj[0]
@@ -66,15 +90,22 @@
         jnp.bfloat16
     )
     slot_gate = lax.psum(gate_terms, "tensor").astype(jnp.bfloat16)
-    back_rows, back_gate = (
-        lax.all_to_all(routed_grad, ("dp", "expert"), split_axis=0, concat_axis=0, tiled=True),
-        lax.all_to_all(slot_gate, ("dp", "expert"), split_axis=0, concat_axis=0, tiled=True),
+
+    back_rows = lax.all_to_all(routed_grad, "expert", split_axis=0, concat_axis=0, tiled=True)
+    back_gate = lax.all_to_all(slot_gate, "expert", split_axis=0, concat_axis=0, tiled=True)
+
+    col_grad = lax.dot_general(
+        select, back_rows, (((0,), (0,)), ((), ())), preferred_element_type=jnp.float32
     )
-    picked = (
-        back_rows[slot_index].astype(jnp.float32).reshape(tok_rows, top_count, back_rows.shape[1])
+    token_grad = lax.psum_scatter(col_grad, "dp", scatter_dimension=0, tiled=True).astype(
+        jnp.bfloat16
     )
-    token_grad = jnp.sum(picked, axis=1).astype(jnp.bfloat16)
-    gate_grad = back_gate[slot_index].reshape(tok_rows, top_count)
+    col_gate = jnp.sum(
+        jnp.where(match, back_gate.astype(jnp.float32)[:, None, None], 0.0), axis=0
+    )
+    gate_grad = lax.psum_scatter(col_gate, "dp", scatter_dimension=0, tiled=True).astype(
+        jnp.bfloat16
+    )
     return (token_grad, gate_grad, grad_g[None], grad_u[None], grad_d[None])
 
 

time: 392 us -> 314 us (0.80); the launches traced: 386 us -> 314 us
  local copies, waits for them, and re-layouts: 43.2 us -> 3.91 us
  starting transfers between devices: 41.4 us -> 8.28 us
  blocking collectives: 114 us -> 96.9 us
  other arithmetic: 21.8 us -> 38.3 us
    all_to_all x4 -> x2, waiting for transfers between devices: 101 us -> 27.1 us  [the longest x1 27.1 us: on_device(): lax.all_to_all(routed_grad, 'expert', split_axis=0, concat_axis=0, tiled=...]
    all_to_all x1 -> x2, blocking collectives: 112 us -> 66.2 us  [the longest x1 57.6 us: on_device(): lax.all_to_all(send, 'expert', split_axis=0, concat_axis=0, tiled=True)]
    all_gather x0 -> x2, waiting for transfers between devices: none -> 39.2 us  [the longest x1 20.3 us: on_device(): carried_all = lax.all_gather(carried, 'dp', tiled=True)]
    gather x5 -> x0, local copies, waits for them, and re-layouts: 34 us -> none  [the longest x1 8.12 us: on_device(): back_rows[slot_index].astype(jnp.float32)]
    all_to_all x4 -> x2, starting transfers between devices: 41.2 us -> 7.89 us  [the longest x1 3.99 us: on_device(): lax.all_to_all(routed_grad, 'expert', split_axis=0, concat_axis=0, tiled=...]
    all_gather x0 -> x2, blocking collectives: none -> 28.2 us  [the longest x1 16.3 us: on_device(): ids_all = lax.all_gather(route_ids, 'dp', tiled=True)]
    reduce_scatter x0 -> x2, waiting for transfers between devices: none -> 25.6 us  [the longest x1 25.6 us: on_device(): lax.psum_scatter(col_grad, 'dp', scatter_dimension=0, tiled=True)]
    reduce_sum x2, other arithmetic: 3.75 us -> 24.1 us  [the longest x1 12.2 us: on_device(): select = jnp.sum(match.astype(jnp.bfloat16), axis=2)]
  transfers between devices with their start and end apart: 5 -> 7, of which waited for: 3 -> 5; matrix products, arithmetic and copies ran while one was open for 15% -> 11% of each run, Pallas kernels for 0% -> 0%
where the time goes in v1:
time: 314 us
  waiting for transfers between devices  108 us (34%)
  blocking collectives  96.9 us (31%)
  matrix products  44 us (14%)
  other arithmetic  38.3 us (12%)
  between operations  14 us (4%)
  starting transfers between devices  8.28 us (3%)
  local copies, waits for them, and re-layouts  3.91 us (1%)
    all_to_all x1, blocking collectives, on_device(): lax.all_to_all(send, 'expert', split_axis=0, concat_axis=0, tiled=True)  57.6 us
    all_to_all x1, waiting for transfers between devices, on_device(): lax.all_to_all(routed_grad, 'expert', split_axis=0, concat_axis=0, tiled=...  27.1 us
    reduce_scatter x1, waiting for transfers between devices, on_device(): lax.psum_scatter(col_grad, 'dp', scatter_dimension=0, tiled=True)  25.6 us
    all_gather x1, waiting for transfers between devices, on_device(): carried_all = lax.all_gather(carried, 'dp', tiled=True)  20.3 us
    all_gather x1, waiting for transfers between devices, on_device(): both = lax.all_gather(recv, 'tensor')  18.9 us
    all_gather x1, blocking collectives, on_device(): ids_all = lax.all_gather(route_ids, 'dp', tiled=True)  16.3 us
    reduce_scatter x1, waiting for transfers between devices, on_device(): lax.psum_scatter(partial_value, 'tensor', scatter_dimension=1, tiled=True)  15.8 us
    reduce_sum x1, other arithmetic, on_device(): select = jnp.sum(match.astype(jnp.bfloat16), axis=2)  12.2 us
  transfers between devices with their start and end apart: 7, of which 5 were waited for; matrix products, arithmetic and copies ran while one was open for 11% of the time, Pallas kernels for 0%

profile of v1, /device:TPU:0, one launch (start us, length us, event | category | flops | bytes accessed | tf_op | source)
XLA Modules:
  0.0 313.8 jit_solution(6951644346922703783)
XLA Ops:
  7.2 0.0 copy-start
  7.2 0.0 all-gather.3.cloned.1.call-start
  7.2 2.0 broadcast_select_fusion
  9.2 0.0 all-gather.3.cloned.1.call-update
  9.3 0.0 all-gather.5.cloned.1.call-start
  9.3 0.1 copy.20
  9.4 16.3 %all_gather.15 = s32[512,8]{1,0:T(8,128)S(1)} all-gather(s32[128,8]{1,0:T(8,128)S(1)} %copy.20), channel_id=1, replica_groups=mesh['dp'=4,'expert'=4,'tensor'=2] {'dp'}, dimensions={0}, use_global_device_ids=true | all-gather | bytes 20480 | tf_op jit(solution)/shard_map/all_gather | solution.py:20
  25.7 0.2 sub.20
  25.9 0.5 fusion.32
  26.4 0.2 convert_element_type.93
  26.6 0.1 broadcast_bitcast_fusion
  26.7 0.1 add_select_fusion
  26.8 0.1 copy.21
  26.9 12.2 %fusion.1 = bf16[1152,512]{1,0:T(8,128)(2,1)S(1)} fusion(s32[512,8]{0,1:T(8,128)S(1)} %copy.21), kind=kLoop, calls=%fused_computation.5 | loop fusion | flops 13565952 | bytes 1196032 | tf_op jit(solution)/shard_map/reduce_sum | solution.py:44
  39.1 0.0 copy-start.2
  39.1 20.3 %all-gather.3.cloned.1.call-done = bf16[512,2048]{1,0:T(8,128)(2,1)} async-done(((bf16[128,2048]{1,0:T(8,128)(2,1)}), bf16[512,2048]{1,0:T(8,128)(2,1)}) %all-gather.3.cloned.1.call-update) | async-done | bytes 2097168 | tf_op jit(solution)/shard_map/all_gather | solution.py:24
  59.4 4.4 %convolution_convert_fusion = bf16[1152,2048]{1,0:T(8,128)(2,1)S(1)} fusion(bf16[1152,512]{1,0:T(8,128)(2,1)S(1)} %fusion.1, bf16[512,2048]{1,0:T(8,128)(2,1)} %all-gather.3.cloned.1.call-done), kind=kOutput, calls=%fused_computation.6 | convolution fusion | flops 2418278400 | bytes 7995392 | tf_op jit(solution)/shard_map/dot_general | solution.py:45
  63.9 57.6 %all_to_all.37 = bf16[4,288,2048]{2,1,0:T(8,128)(2,1)} all-to-all(bf16[4,288,2048]{2,1,0:T(8,128)(2,1)S(1)} %bitcast.82), channel_id=1, replica_groups=mesh['dp'=4,'expert'=4,'tensor'=2] {'expert'}, dimensions={0} | all-to-all | bytes 9437184 | tf_op jit(solution)/shard_map/all_to_all | solution.py:50
  121.4 0.0 all-gather.5.cloned.1.call-update
  121.5 0.0 copy-start.7
  121.5 18.9 %all-gather.5.cloned.1.call-done = bf16[2,1152,2048]{2,1,0:T(8,128)(2,1)} async-done(((bf16[1,1152,2048]{2,1,0:T(8,128)(2,1)}), bf16[2,1152,2048]{2,1,0:T(8,128)(2,1)}) %all-gather.5.cloned.1.call-update) | async-done | bytes 9437200 | tf_op jit(solution)/shard_map/all_gather | solution.py:52
  140.4 4.8 %fusion.9 = f32[1152,384]{0,1:T(8,128)S(1)} fusion(bf16[2,1152,2048]{2,1,0:T(8,128)(2,1)} %all-gather.5.cloned.1.call-done, bf16[1,2048,384]{2,1,0:T(8,128)(2,1)S(1)} %copy-done), kind=kOutput, calls=%fused_computation.16 | convolution fusion | flops 1811939328 | bytes 8060928 | tf_op jit(solution)/shard_map/dot_general | solution.py:59
  145.2 0.3 copy-done.11
  145.5 2.4 fusion.10
  147.9 0.0 copy-start.10
  147.9 3.8 %fusion.17 = (f32[1152]{0:T(1024)S(1)}, bf16[1152,384]{0,1:T(8,128)(2,1)}, f32[1152,384]{0,1:T(8,128)}) fusion(f32[1152,384]{0,1:T(8,128)S(1)} %fusion.10, f32[1152,384]{0,1:T(8,128)S(1)} %fusion.9, bf16[1,384,2048]{2,1,0:T(8,128)(2,1)S(1)} %copy-done.12, bf16[2,1152,2048]{2,1,0:T(8,128)(2,1)S(1)} %copy-done.11), kind=kOutput, calls=%fused_computation.26 | convolution fusion | flops 1815919488 | bytes 12489216 | tf_op jit(solution)/shard_map/dot_general | solution.py:64
  151.8 2.5 psum.7
  154.3 0.1 all_to_all.32
  154.4 0.5 broadcast.52
  154.9 0.7 reduce.5
  155.5 0.7 reshape.85
  156.2 3.9 %all-to-all-start.3 = ((bf16[4,2,144]{2,1,0:T(2,128)(2,1)}), bf16[4,2,144]{2,1,0:T(2,128)(2,1)S(1)}, u32[]{:S(2)}, u32[]{:S(2)}) async-start(bf16[4,2,144]{2,1,0:T(2,128)(2,1)} %reshape.85), calls=%async_computation.5 | async-start | bytes 8192 | tf_op jit(solution)/shard_map/all_to_all | solution.py:95
  160.1 11.9 %all_gather.16 = bf16[512,8]{0,1:T(8,128)(2,1)S(1)} all-gather(bf16[128,8]{0,1:T(8,128)(2,1)S(1)} %copy-done.10), channel_id=1, replica_groups=mesh['dp'=4,'expert'=4,'tensor'=2] {'dp'}, dimensions={0}, use_global_device_ids=true | all-gather | bytes 10240 | tf_op jit(solution)/shard_map/all_gather | solution.py:21
  172.1 0.1 reshape.86
  172.2 0.1 reshape.81
  172.3 11.9 %select_reduce_fusion = (f32[512,8]{0,1:T(8,128)}, bf16[1152]{0:T(1024)(128)(2,1)S(1)}) fusion(f32[1152]{0:T(1024)S(1)} %reshape.81, s32[512,8]{0,1:T(8,128)S(1)} %copy.21, f32[512,8]{0,1:T(8,128)S(1)} %convert_element_type.95), kind=kLoop, calls=%fused_computation | loop fusion | flops 23587712 | bytes 56064 | tf_op jit(solution)/shard_map/reduce_sum | solution.py:103
  184.2 0.1 convert_element_type.117
  184.3 0.7 reduce.6
  185.0 0.1 reshape.87
  185.0 8.6 %all_to_all.38 = bf16[4,2,144]{2,1,0:T(2,128)(2,1)S(1)} all-to-all(bf16[4,2,144]{2,1,0:T(2,128)(2,1)S(1)} %reshape.87), channel_id=1, replica_groups=mesh['dp'=4,'expert'=4,'tensor'=2] {'expert'}, dimensions={0} | all-to-all | bytes 4608 | tf_op jit(solution)/shard_map/all_to_all | solution.py:51
  193.7 0.1 reshape.88
  193.8 0.1 reshape.80
  193.9 3.4 %multiply_convert_fusion.1 = (bf16[1152,384]{0,1:T(8,128)(2,1)S(1)}, bf16[1152,384]{0,1:T(8,128)(2,1)S(1)}) fusion(f32[1152,384]{0,1:T(8,128)} %get-tuple-element.11, f32[1152]{0:T(1024)S(1)} %reshape.80, f32[1152,384]{0,1:T(8,128)} %copy-done.5, f32[1152,384]{0,1:T(8,128)} %copy-done.6), kind=kLoop, calls=%fused_computation.29 | loop fusion | flops 6193152 | bytes 7082496 | tf_op jit(solution)/shard_map/convert_element_type | solution.py:70
  197.3 0.0 copy-start.3
  197.3 0.0 copy-start.8
  197.3 2.7 fusion.20
  200.0 5.1 %convolution_add_fusion = f32[1152,2048]{1,0:T(8,128)} fusion(f32[1152,2048]{1,0:T(8,128)S(1)} %fusion.20, bf16[1152,384]{0,1:T(8,128)(2,1)S(1)} %get-tuple-element.9, bf16[1,2048,384]{2,1,0:T(8,128)(2,1)S(1)} %copy-done.8), kind=kOutput, calls=%fused_computation.4 | convolution fusion | flops 1814298624 | bytes 21331968 | tf_op jit(solution)/shard_map/dot_general | solution.py:86
  205.2 0.0 reduce-scatter.4.cloned.1.call-update
  205.2 15.8 %reduce-scatter.4.cloned.1.call-done = f32[1152,1024]{1,0:T(8,128)} async-done(((f32[1152,2048]{1,0:T(8,128)}), f32[1152,1024]{1,0:T(8,128)}) %reduce-scatter.4.cloned.1.call-update) | async-done | bytes 4718608 | tf_op jit(solution)/shard_map/reduce_scatter | solution.py:89
  221.0 4.1 %convert_element_type.103 = bf16[1152,1024]{1,0:T(8,128)(2,1)} convert(f32[1152,1024]{1,0:T(8,128)} %reduce-scatter.4.cloned.1.call-done) | non-fusion elementwise | flops 1179648 | bytes 7077888 | tf_op jit(solution)/shard_map/convert_element_type | solution.py:89
  225.1 4.0 %all-to-all-start.2 = ((bf16[4,288,1024]{2,1,0:T(8,128)(2,1)}), bf16[4,288,1024]{2,1,0:T(8,128)(2,1)S(1)}, u32[]{:S(2)}, u32[]{:S(2)}) async-start(bf16[4,288,1024]{2,1,0:T(8,128)(2,1)} %bitcast.10), calls=%async_computation.3 | async-start | bytes 4718592 | tf_op jit(solution)/shard_map/all_to_all | solution.py:94
  229.1 0.6 reduce-scatter.8.cloned.1.call-update
  229.7 0.3 reduce-scatter.6.cloned.1.call-start
  230.0 27.1 %all-to-all-done.2 = bf16[4,288,1024]{2,1,0:T(8,128)(2,1)S(1)} async-done(((bf16[4,288,1024]{2,1,0:T(8,128)(2,1)}), bf16[4,288,1024]{2,1,0:T(8,128)(2,1)S(1)}, u32[]{:S(2)}, u32[]{:S(2)}) %all-to-all-start.2) | async-done | bytes 2359328 | tf_op jit(solution)/shard_map/all_to_all | solution.py:94
  257.1 4.1 %fusion.38 = f32[512,1024]{1,0:T(8,128)} fusion(bf16[1152,512]{1,0:T(8,128)(2,1)} %copy-done.2, bf16[1152,1024]{1,0:T(8,128)(2,1)S(1)} %bitcast.81), kind=kOutput, calls=%fused_computation.52 | convolution fusion | flops 1207959552 | bytes 5636096 | tf_op jit(solution)/shard_map/dot_general | solution.py:97
  261.2 0.0 reduce-scatter.6.cloned.1.call-update
  261.2 1.1 copy-done.13
  262.4 5.8 %fusion.14 = bf16[1,384,2048]{2,1,0:T(8,128)(2,1)} fusion(bf16[2,1152,2048]{2,1,0:T(8,128)(2,1)} %all-gather.5.cloned.1.call-done, bf16[1152,384]{0,1:T(8,128)(2,1)S(1)} %copy-done.13, f32[1152]{0:T(1024)S(1)} %reshape.80), kind=kOutput, calls=%fused_computation.21 | convolution fusion | flops 1814052864 | bytes 7180800 | tf_op jit(solution)/shard_map/dot_general | solution.py:81
  268.2 6.4 %fusion.15 = bf16[1,2048,384]{2,1,0:T(8,128)(2,1)} fusion(bf16[1152,384]{0,1:T(8,128)(2,1)S(1)} %get-tuple-element.9, bf16[2,1152,2048]{2,1,0:T(8,128)(2,1)} %all-gather.5.cloned.1.call-done), kind=kOutput, calls=%fused_computation.22 | convolution fusion | flops 1812725760 | bytes 7176192 | tf_op jit(solution)/shard_map/dot_general | solution.py:77
  274.7 0.0 copy-start.1
  274.7 3.9 %fusion.16 = bf16[1,2048,384]{2,1,0:T(8,128)(2,1)} fusion(bf16[1152,384]{0,1:T(8,128)(2,1)S(1)} %copy-done.4, bf16[2,1152,2048]{2,1,0:T(8,128)(2,1)S(1)} %bitcast.86), kind=kOutput, calls=%fused_computation.23 | convolution fusion | flops 1812725760 | bytes 7176192 | tf_op jit(solution)/shard_map/dot_general | solution.py:74
  278.6 1.3 convert_element_type.110
  279.9 25.6 %reduce-scatter.6.cloned.1.call-done = f32[128,1024]{1,0:T(8,128)} async-done(((f32[512,1024]{1,0:T(8,128)}), f32[128,1024]{1,0:T(8,128)}) %reduce-scatter.6.cloned.1.call-update) | async-done | bytes 524304 | tf_op jit(solution)/shard_map/reduce_scatter | solution.py:100
  305.5 1.8 convert_element_type.104
  (36 shorter events, 0.2 us)
Async XLA Ops:
  7.2 133.2 %copy-start = (bf16[1,2048,384]{2,1,0:T(8,128)(2,1)S(1)}, bf16[1,2048,384]{2,1,0:T(8,128)(2,1)}, u32[]{:S(2)}) copy-start(bf16[1,2048,384]{2,1,0:T(8,128)(2,1)} %param.11) | copy-start | bytes 4718596
  7.2 2.1 copy-start.9
  7.2 52.2 %all-gather.3.cloned.1.call-start = ((), (), s32[]{:S(2)}) async-start(), calls=%async_computation.7 | async-start | bytes 2621440 | tf_op jit(solution)/shard_map/all_gather | solution.py:24
  9.3 131.1 %all-gather.5.cloned.1.call-start = ((), (), s32[]{:S(2)}) async-start(), calls=%async_computation.8 | async-start | bytes 14155776 | tf_op jit(solution)/shard_map/all_gather | solution.py:52
  39.1 24.7 %copy-start.2 = (bf16[1152,512]{1,0:T(8,128)(2,1)}, bf16[1152,512]{1,0:T(8,128)(2,1)S(1)}, u32[]{:S(2)}) copy-start(bf16[1152,512]{1,0:T(8,128)(2,1)S(1)} %fusion.1) | copy-start | bytes 3538948
  121.5 23.7 %copy-start.7 = (bf16[1,2048,384]{2,1,0:T(8,128)(2,1)S(1)}, bf16[1,2048,384]{2,1,0:T(8,128)(2,1)}, u32[]{:S(2)}) copy-start(bf16[1,2048,384]{2,1,0:T(8,128)(2,1)} %param.12) | copy-start | bytes 4718596
  140.4 5.1 %copy-start.11 = (bf16[2,1152,2048]{2,1,0:T(8,128)(2,1)S(1)}, bf16[2,1152,2048]{2,1,0:T(8,128)(2,1)}, u32[]{:S(2)}) copy-start(bf16[2,1152,2048]{2,1,0:T(8,128)(2,1)} %all-gather.5.cloned.1.call-done) | copy-start | bytes 28311556
  145.5 2.4 copy-start.5
  145.5 2.4 copy-start.12
  147.9 3.9 %copy-start.6 = (f32[1152,384]{0,1:T(8,128)}, f32[1152,384]{0,1:T(8,128)S(1)}, u32[]{:S(2)}) copy-start(f32[1152,384]{0,1:T(8,128)S(1)} %fusion.10) | copy-start | bytes 5308420
  147.9 12.2 %copy-start.10 = (bf16[128,8]{0,1:T(8,128)(2,1)S(1)}, bf16[128,8]{0,1:T(8,128)(2,1)}, u32[]{:S(2)}) copy-start(bf16[128,8]{0,1:T(8,128)(2,1)} %param.10) | copy-start | bytes 6148
  156.2 15.8 %all-to-all-start.3 = ((bf16[4,2,144]{2,1,0:T(2,128)(2,1)}), bf16[4,2,144]{2,1,0:T(2,128)(2,1)S(1)}, u32[]{:S(2)}, u32[]{:S(2)}) async-start(bf16[4,2,144]{2,1,0:T(2,128)(2,1)} %reshape.85), calls=%async_computation.5 | async-start | bytes 8192 | tf_op jit(solution)/shard_map/all_to_all | solution.py:95
  160.1 60.9 %reduce-scatter.4.cloned.1.call-start = ((), (), s32[]{:S(2)}) async-start(), calls=%async_computation.9 | async-start | bytes 14155776 | tf_op jit(solution)/shard_map/reduce_scatter | solution.py:89
  197.3 2.7 copy-start.3
  197.3 2.7 copy-start.8
  225.1 32.0 %all-to-all-start.2 = ((bf16[4,288,1024]{2,1,0:T(8,128)(2,1)}), bf16[4,288,1024]{2,1,0:T(8,128)(2,1)S(1)}, u32[]{:S(2)}, u32[]{:S(2)}) async-start(bf16[4,288,1024]{2,1,0:T(8,128)(2,1)} %bitcast.10), calls=%async_computation.3 | async-start | bytes 4718592 | tf_op jit(solution)/shard_map/all_to_all | solution.py:94
  229.1 49.5 %reduce-scatter.8.cloned.1.call-start = ((), (), s32[]{:S(2)}) async-start(), calls=%async_computation.11 | async-start | bytes 20480 | tf_op jit(solution)/shard_map/reduce_scatter | solution.py:106
  229.7 75.8 %reduce-scatter.6.cloned.1.call-start = ((), (), s32[]{:S(2)}) async-start(), calls=%async_computation.10 | async-start | bytes 2621440 | tf_op jit(solution)/shard_map/reduce_scatter | solution.py:100
  261.2 1.2 copy-start.13
  262.4 12.3 %slice-start = ((s8[9437184]{0:T(1024)(128)(4,1)}), s8[4194304]{0:T(1024)(128)(4,1)S(1)}, s32[]{:S(2)}) async-start(s8[9437184]{0:T(1024)(128)(4,1)} %bitcast.85), calls=%async_computation.12 | async-start | bytes 8388608
  262.4 12.3 %slice-start.1 = ((s8[9437184]{0:T(1024)(128)(4,1)}), s8[4194304]{0:T(1024)(128)(4,1)S(1)}, s32[]{:S(2)}) async-start(s8[9437184]{0:T(1024)(128)(4,1)} %bitcast.85), calls=%async_computation.13 | async-start | bytes 8388608
  268.2 6.4 %copy-start.4 = (bf16[1152,384]{0,1:T(8,128)(2,1)S(1)}, bf16[1152,384]{0,1:T(8,128)(2,1)}, u32[]{:S(2)}) copy-start(bf16[1152,384]{0,1:T(8,128)(2,1)} %copy-done.3) | copy-start | bytes 2654212
  268.2 6.4 %slice-start.2 = ((s8[9437184]{0:T(1024)(128)(4,1)}), s8[1048576]{0:T(1024)(128)(4,1)S(1)}, s32[]{:S(2)}) async-start(s8[9437184]{0:T(1024)(128)(4,1)} %bitcast.85), calls=%async_computation.14 | async-start | bytes 2097152
  274.7 32.6 %copy-start.1 = (bf16[1,2048,384]{2,1,0:T(8,128)(2,1)S(1)}, bf16[1,2048,384]{2,1,0:T(8,128)(2,1)}, u32[]{:S(2)}) copy-start(bf16[1,2048,384]{2,1,0:T(8,128)(2,1)} %param.11) | copy-start | bytes 4718596
Sparse Core Ops, SparseCore 0:
  10.2 49.2 all-gather.2
  121.6 18.7 all-gather.4
  205.3 15.6 reduce-scatter.3
  232.4 20.2 reduce-scatter.7
  261.4 44.0 reduce-scatter.5

commit v2 on v1

--- a/solution.py
+++ b/solution.py
@@ -14,14 +14,16 @@
     plane = lax.axis_index("dp")
     core = lax.axis_index("tensor")
     col_rows = n_dp * tok_rows
-    plane_slots = n_dp * capacity
-    slots = n_ex * plane_slots
-
-    ids_all = lax.all_gather(route_ids, "dp", tiled=True)
-    gates_all = lax.all_gather(gate_values, "dp", tiled=True)
+    slots = n_ex * n_dp * capacity
 
     carried = jnp.where(core == 0, tokens, grad_out)
-    carried_all = lax.all_gather(carried, "dp", tiled=True)
+    aux = jnp.concatenate([route_ids.astype(tokens.dtype), gate_values.astype(tokens.dtype)], axis=1)
+    pad = (-(features + aux.shape[1])) % 128
+    aux = jnp.pad(aux, ((0, 0), (0, pad)))
+    ext_all = lax.all_gather(jnp.concatenate([carried, aux], axis=1), "dp", tiled=True)
+    carried_all = ext_all[:, :features].reshape(n_dp, tok_rows, features)
+    ids_all = ext_all[:, features:features + top_count].astype(jnp.int32)
+    gates_all = ext_all[:, features + top_count:features + 2 * top_count].astype(jnp.float32)
 
     routes = tok_rows * top_count
     ids_blk = ids_all.reshape(n_dp, routes)
@@ -35,20 +37,26 @@
         "ab,nbe->nae", earlier, one_hot_b, preferred_element_type=jnp.float32
     )
     position = jnp.sum(running * one_hot.astype(jnp.float32), axis=2).astype(jnp.int32)
-    blk = jnp.arange(n_dp, dtype=jnp.int32)[:, None]
-    slot_of = jnp.where(in_plane, local_ex * plane_slots + blk * capacity + position, -1)
-    slot_of = slot_of.reshape(col_rows, top_count)
+    key = jnp.where(in_plane, local_ex * capacity + position, -1)
+    key = key.reshape(n_dp, tok_rows, top_count)
 
-    s_iota = jnp.arange(slots, dtype=jnp.int32)
-    match = slot_of[None, :, :] == s_iota[:, None, None]
-    select = jnp.sum(match.astype(jnp.bfloat16), axis=2)
-    send = jnp.dot(select, carried_all, preferred_element_type=jnp.float32).astype(tokens.dtype)
-    send_gate = jnp.sum(
-        jnp.where(match, gates_all.astype(jnp.float32)[None, :, :], 0.0), axis=(1, 2)
-    ).astype(gate_values.dtype)
+    q_iota = jnp.arange(n_ex * capacity, dtype=jnp.int32)
+    match = key[:, None, :, :] == q_iota[None, :, None, None]
+    select = jnp.sum(match.astype(jnp.bfloat16), axis=3)
+    gates_blk = gates_all.reshape(n_dp, tok_rows, top_count)
+    send = jnp.einsum(
+        "bqt,btf->bqf", select, carried_all, preferred_element_type=jnp.float32
+    ).astype(tokens.dtype)
+    send_gate = jnp.sum(jnp.where(match, gates_blk[:, None, :, :], 0.0), axis=(2, 3)).astype(
+        gate_values.dtype
+    )
 
-    recv = lax.all_to_all(send, "expert", split_axis=0, concat_axis=0, tiled=True)
-    routed_gate = lax.all_to_all(send_gate, "expert", split_axis=0, concat_axis=0, tiled=True)
+    recv = lax.all_to_all(
+        send.reshape(n_dp, n_ex, capacity, features), "expert", split_axis=1, concat_axis=1, tiled=True
+    ).reshape(slots, features)
+    routed_gate = lax.all_to_all(
+        send_gate.reshape(n_dp, n_ex, capacity), "expert", split_axis=1, concat_axis=1, tiled=True
+    ).reshape(slots)
     both = lax.all_gather(recv, "tensor")
     routed_x = both[0]
     routed_dy = both[1]
@@ -91,18 +99,23 @@
     )
     slot_gate = lax.psum(gate_terms, "tensor").astype(jnp.bfloat16)
 
-    back_rows = lax.all_to_all(routed_grad, "expert", split_axis=0, concat_axis=0, tiled=True)
-    back_gate = lax.all_to_all(slot_gate, "expert", split_axis=0, concat_axis=0, tiled=True)
+    half = routed_grad.shape[1]
+    back_rows = lax.all_to_all(
+        routed_grad.reshape(n_dp, n_ex, capacity, half), "expert", split_axis=1, concat_axis=1, tiled=True
+    ).reshape(n_dp, n_ex * capacity, half)
+    back_gate = lax.all_to_all(
+        slot_gate.reshape(n_dp, n_ex, capacity), "expert", split_axis=1, concat_axis=1, tiled=True
+    ).reshape(n_dp, n_ex * capacity)
 
-    col_grad = lax.dot_general(
-        select, back_rows, (((0,), (0,)), ((), ())), preferred_element_type=jnp.float32
-    )
+    col_grad = jnp.einsum(
+        "bqt,bqf->btf", select, back_rows, preferred_element_type=jnp.float32
+    ).reshape(col_rows, half)
     token_grad = lax.psum_scatter(col_grad, "dp", scatter_dimension=0, tiled=True).astype(
         jnp.bfloat16
     )
     col_gate = jnp.sum(
-        jnp.where(match, back_gate.astype(jnp.float32)[:, None, None], 0.0), axis=0
-    )
+        jnp.where(match, back_gate.astype(jnp.float32)[:, :, None, None], 0.0), axis=1
+    ).reshape(col_rows, top_count)
     gate_grad = lax.psum_scatter(col_gate, "dp", scatter_dimension=0, tiled=True).astype(
         jnp.bfloat16
     )

time: 314 us -> 310 us (0.987)
  waiting for transfers between devices: 108 us -> 145 us
  blocking collectives: 96.9 us -> 66.3 us
  other arithmetic: 38.3 us -> 26.6 us
  local copies, waits for them, and re-layouts: 3.91 us -> 10.9 us
  matrix products: 44 us -> 39 us
    all_gather x1, waiting for transfers between devices: 20.3 us -> 51.1 us  [on_device(): lax.all_gather(jnp.concatenate([carried, aux], axis=1), 'dp', tiled=True)]
    all_gather x2 -> x0, blocking collectives: 28.2 us -> none  [the longest x1 16.3 us: on_device(): ids_all = lax.all_gather(route_ids, 'dp', tiled=True)]
    reduce_sum x2, other arithmetic: 24.1 us -> 12.1 us  [the longest x1 9.89 us: on_device(): jnp.sum(jnp.where(match, back_gate.astype(jnp.float32)[:, :, None, None],...]
    dot_general x2, matrix products: 8.52 us -> 3.45 us  [the longest x1 2.07 us: on_device(): jnp.einsum('bqt,bqf->btf', select, back_rows, preferred_element_type=jnp....]
    all_to_all x2, waiting for transfers between devices: 27.1 us -> 30.8 us  [the longest x1 27.2 us: on_device(): lax.all_to_all(routed_grad.reshape(n_dp, n_ex, capacity, half), 'expert',...]
  transfers between devices with their start and end apart: 7 -> 7, of which waited for: 5 -> 6; matrix products, arithmetic and copies ran while one was open for 11% -> 7% of each run, Pallas kernels for 0% -> 0%
where the time goes in v2:
time: 310 us
  waiting for transfers between devices  145 us (47%)
  blocking collectives  66.3 us (21%)
  matrix products  39 us (13%)
  other arithmetic  26.6 us (9%)
  between operations  14 us (5%)
  local copies, waits for them, and re-layouts  10.9 us (4%)
  starting transfers between devices  8.25 us (3%)
    all_to_all x1, blocking collectives, on_device(): lax.all_to_all(send.reshape(n_dp, n_ex, capacity, features), 'expert', sp...  56.9 us
    all_gather x1, waiting for transfers between devices, on_device(): lax.all_gather(jnp.concatenate([carried, aux], axis=1), 'dp', tiled=True)  51.1 us
    all_to_all x1, waiting for transfers between devices, on_device(): lax.all_to_all(routed_grad.reshape(n_dp, n_ex, capacity, half), 'expert',...  27.2 us
    reduce_scatter x1, waiting for transfers between devices, on_device(): lax.psum_scatter(col_grad, 'dp', scatter_dimension=0, tiled=True)  25.5 us
    all_gather x1, waiting for transfers between devices, on_device(): both = lax.all_gather(recv, 'tensor')  19.5 us
    reduce_scatter x1, waiting for transfers between devices, on_device(): lax.psum_scatter(partial_value, 'tensor', scatter_dimension=1, tiled=True)  17 us
    reduce_sum x1, other arithmetic, on_device(): jnp.sum(jnp.where(match, back_gate.astype(jnp.float32)[:, :, None, None],...  9.89 us
    all_to_all x1, blocking collectives, on_device(): lax.all_to_all(send_gate.reshape(n_dp, n_ex, capacity), 'expert', split_a...  7 us
  transfers between devices with their start and end apart: 7, of which 6 were waited for; matrix products, arithmetic and copies ran while one was open for 7% of the time, Pallas kernels for 0%

profile of v2, /device:TPU:0, one launch (start us, length us, event | category | flops | bytes accessed | tf_op | source)
XLA Modules:
  0.0 309.8 jit_solution(5270696314553862138)
XLA Ops:
  7.2 0.0 copy-start
  7.2 0.0 all-gather.3.cloned.1.call-start
  7.2 0.8 convert_element_type.94
  8.0 0.7 pad_maximum_fusion
  8.7 0.1 copy.38
  8.8 1.1 broadcast_select_fusion
  9.9 0.8 fusion.38
  10.8 0.0 all-gather.3.cloned.1.call-update
  10.8 0.0 all-gather.5.cloned.1.call-start
  10.9 51.1 %all-gather.3.cloned.1.call-done = bf16[512,2176]{1,0:T(8,128)(2,1)} async-done(((bf16[128,2176]{1,0:T(8,128)(2,1)}), bf16[512,2176]{1,0:T(8,128)(2,1)}) %all-gather.3.cloned.1.call-update) | async-done | bytes 2228240 | tf_op jit(solution)/shard_map/all_gather | solution.py:23
  62.0 0.9 convert_subtract_fusion
  63.0 0.2 sub.23
  63.1 0.5 fusion.32
  63.7 0.2 convert_element_type.97
  63.8 1.0 compare_and_fusion
  64.9 0.1 copy.28
  65.0 2.2 fusion.16
  67.1 1.6 slice-done
  68.7 1.4 convolution_convert_fusion
  70.1 0.7 copy.32
  70.8 56.9 %all_to_all.20 = bf16[4,4,72,2048]{3,2,0,1:T(8,128)(2,1)S(1)} all-to-all(bf16[4,4,72,2048]{3,2,0,1:T(8,128)(2,1)S(1)} %copy.32), channel_id=1, replica_groups=mesh['dp'=4,'expert'=4,'tensor'=2] {'expert'}, dimensions={1} | all-to-all | bytes 9437184 | tf_op jit(solution)/shard_map/all_to_all | solution.py:54
  127.7 2.6 copy.33
  130.3 0.0 all-gather.5.cloned.1.call-update
  130.3 0.0 copy-start.6
  130.3 19.5 %all-gather.5.cloned.1.call-done = bf16[2,1152,2048]{2,1,0:T(8,128)(2,1)} async-done(((bf16[1,1152,2048]{2,1,0:T(8,128)(2,1)}), bf16[2,1152,2048]{2,1,0:T(8,128)(2,1)}) %all-gather.5.cloned.1.call-update) | async-done | bytes 9437200 | tf_op jit(solution)/shard_map/all_gather | solution.py:60
  149.8 4.8 %fusion.8 = f32[1152,384]{0,1:T(8,128)S(1)} fusion(bf16[2,1152,2048]{2,1,0:T(8,128)(2,1)} %all-gather.5.cloned.1.call-done, bf16[1,2048,384]{2,1,0:T(8,128)(2,1)S(1)} %copy-done), kind=kOutput, calls=%fused_computation.15 | convolution fusion | flops 1811939328 | bytes 8060928 | tf_op jit(solution)/shard_map/dot_general | solution.py:67
  154.6 0.3 copy-done.8
  154.9 2.4 fusion.9
  157.4 3.8 %fusion.17 = (f32[1152]{0:T(1024)S(1)}, bf16[1152,384]{0,1:T(8,128)(2,1)}, f32[1152,384]{0,1:T(8,128)}) fusion(f32[1152,384]{0,1:T(8,128)S(1)} %fusion.9, f32[1152,384]{0,1:T(8,128)S(1)} %fusion.8, bf16[1,384,2048]{2,1,0:T(8,128)(2,1)S(1)} %copy-done.9, bf16[2,1152,2048]{2,1,0:T(8,128)(2,1)S(1)} %copy-done.8), kind=kOutput, calls=%fused_computation.26 | convolution fusion | flops 1815919488 | bytes 12489216 | tf_op jit(solution)/shard_map/dot_general | solution.py:72
  161.2 2.5 psum.7
  163.7 0.1 reshape.90
  163.8 0.6 copy.36
  164.4 3.9 %all-to-all-start.3 = ((bf16[4,4,72]{2,0,1:T(4,128)(2,1)}), bf16[4,4,72]{2,0,1:T(4,128)(2,1)S(1)}, u32[]{:S(2)}, u32[]{:S(2)}) async-start(bf16[4,4,72]{2,0,1:T(4,128)(2,1)} %copy.36), calls=%async_computation.5 | async-start | bytes 8192 | tf_op jit(solution)/shard_map/all_to_all | solution.py:106
  168.3 1.0 slice.21
  169.3 0.1 copy.29
  169.4 3.6 %all-to-all-done.3 = bf16[4,4,72]{2,0,1:T(4,128)(2,1)S(1)} async-done(((bf16[4,4,72]{2,0,1:T(4,128)(2,1)}), bf16[4,4,72]{2,0,1:T(4,128)(2,1)S(1)}, u32[]{:S(2)}, u32[]{:S(2)}) %all-to-all-start.3) | async-done | bytes 2336 | tf_op jit(solution)/shard_map/all_to_all | solution.py:106
  173.0 0.1 reshape.94
  173.1 9.9 %select_reduce_fusion = (f32[4,128,8]{1,2,0:T(8,128)}, bf16[4,288]{1,0:T(4,128)(2,1)S(1)}) fusion(f32[4,288]{1,0:T(4,128)S(1)} %reshape.94, s32[4,128,8]{1,2,0:T(8,128)S(1)} %copy.28, f32[4,128,8]{1,2,0:T(8,128)S(1)} %copy.29), kind=kLoop, calls=%fused_computation.3 | loop fusion | flops 5892992 | bytes 56064 | tf_op jit(solution)/shard_map/reduce_sum | solution.py:116
  182.9 0.1 convert_element_type.100
  183.0 7.0 %all_to_all.21 = bf16[4,4,72]{2,0,1:T(4,128)(2,1)S(1)} all-to-all(bf16[4,4,72]{2,0,1:T(4,128)(2,1)S(1)} %copy.30), channel_id=1, replica_groups=mesh['dp'=4,'expert'=4,'tensor'=2] {'expert'}, dimensions={1} | all-to-all | bytes 4608 | tf_op jit(solution)/shard_map/all_to_all | solution.py:57
  190.1 0.1 reshape.93
  190.1 3.4 %multiply_convert_fusion.1 = (bf16[1152,384]{0,1:T(8,128)(2,1)S(1)}, bf16[1152,384]{0,1:T(8,128)(2,1)S(1)}) fusion(f32[1152,384]{0,1:T(8,128)} %get-tuple-element.13, f32[1152]{0:T(1024)S(1)} %reshape.93, f32[1152,384]{0,1:T(8,128)} %copy-done.4, f32[1152,384]{0,1:T(8,128)} %copy-done.5), kind=kLoop, calls=%fused_computation.29 | loop fusion | flops 6193152 | bytes 7082496 | tf_op jit(solution)/shard_map/convert_element_type | solution.py:78
  193.6 0.0 copy-start.7
  193.6 2.7 fusion.20
  196.3 5.1 %convolution_add_fusion = f32[1152,2048]{1,0:T(8,128)} fusion(f32[1152,2048]{1,0:T(8,128)S(1)} %fusion.20, bf16[1152,384]{0,1:T(8,128)(2,1)S(1)} %get-tuple-element.9, bf16[1,2048,384]{2,1,0:T(8,128)(2,1)S(1)} %copy-done.7), kind=kOutput, calls=%fused_computation | convolution fusion | flops 1814298624 | bytes 21331968 | tf_op jit(solution)/shard_map/dot_general | solution.py:94
  201.4 0.0 reduce-scatter.4.cloned.1.call-update
  201.4 17.0 %reduce-scatter.4.cloned.1.call-done = f32[1152,1024]{1,0:T(8,128)} async-done(((f32[1152,2048]{1,0:T(8,128)}), f32[1152,1024]{1,0:T(8,128)}) %reduce-scatter.4.cloned.1.call-update) | async-done | bytes 4718608 | tf_op jit(solution)/shard_map/reduce_scatter | solution.py:97
  218.5 2.7 convert_element_type.106
  221.2 1.7 copy.34
  222.9 4.0 %all-to-all-start.2 = ((bf16[4,4,72,1024]{3,2,0,1:T(8,128)(2,1)}), bf16[4,4,72,1024]{3,2,0,1:T(8,128)(2,1)S(1)}, u32[]{:S(2)}, u32[]{:S(2)}) async-start(bf16[4,4,72,1024]{3,2,0,1:T(8,128)(2,1)} %copy.34), calls=%async_computation.3 | async-start | bytes 4718592 | tf_op jit(solution)/shard_map/all_to_all | solution.py:103
  226.8 0.6 reduce-scatter.8.cloned.1.call-update
  227.4 0.3 reduce-scatter.6.cloned.1.call-start
  227.7 27.2 %all-to-all-done.2 = bf16[4,4,72,1024]{3,2,0,1:T(8,128)(2,1)S(1)} async-done(((bf16[4,4,72,1024]{3,2,0,1:T(8,128)(2,1)}), bf16[4,4,72,1024]{3,2,0,1:T(8,128)(2,1)S(1)}, u32[]{:S(2)}, u32[]{:S(2)}) %all-to-all-start.2) | async-done | bytes 2359328 | tf_op jit(solution)/shard_map/all_to_all | solution.py:103
  254.9 0.2 copy.35
  255.2 2.1 fusion.40
  257.3 0.0 reduce-scatter.6.cloned.1.call-update
  257.3 1.1 copy-done.10
  258.4 5.8 %fusion.13 = bf16[1,384,2048]{2,1,0:T(8,128)(2,1)} fusion(bf16[2,1152,2048]{2,1,0:T(8,128)(2,1)} %all-gather.5.cloned.1.call-done, bf16[1152,384]{0,1:T(8,128)(2,1)S(1)} %copy-done.10, f32[1152]{0:T(1024)S(1)} %reshape.93), kind=kOutput, calls=%fused_computation.20 | convolution fusion | flops 1814052864 | bytes 7180800 | tf_op jit(solution)/shard_map/dot_general | solution.py:89
  264.3 6.4 %fusion.14 = bf16[1,2048,384]{2,1,0:T(8,128)(2,1)} fusion(bf16[1152,384]{0,1:T(8,128)(2,1)S(1)} %get-tuple-element.9, bf16[2,1152,2048]{2,1,0:T(8,128)(2,1)} %all-gather.5.cloned.1.call-done), kind=kOutput, calls=%fused_computation.21 | convolution fusion | flops 1812725760 | bytes 7176192 | tf_op jit(solution)/shard_map/dot_general | solution.py:85
  270.7 0.0 copy-start.1
  270.7 3.9 %fusion.15 = bf16[1,2048,384]{2,1,0:T(8,128)(2,1)} fusion(bf16[1152,384]{0,1:T(8,128)(2,1)S(1)} %copy-done.3, bf16[2,1152,2048]{2,1,0:T(8,128)(2,1)S(1)} %bitcast.90), kind=kOutput, calls=%fused_computation.22 | convolution fusion | flops 1812725760 | bytes 7176192 | tf_op jit(solution)/shard_map/dot_general | solution.py:82
  274.7 1.3 convert_element_type.113
  275.9 25.5 %reduce-scatter.6.cloned.1.call-done = f32[128,1024]{1,0:T(8,128)} async-done(((f32[512,1024]{1,0:T(8,128)}), f32[128,1024]{1,0:T(8,128)}) %reduce-scatter.6.cloned.1.call-update) | async-done | bytes 524304 | tf_op jit(solution)/shard_map/reduce_scatter | solution.py:113
  301.5 1.8 convert_element_type.107
  (32 shorter events, 0.1 us)
Async XLA Ops:
  7.2 142.7 %copy-start = (bf16[1,2048,384]{2,1,0:T(8,128)(2,1)S(1)}, bf16[1,2048,384]{2,1,0:T(8,128)(2,1)}, u32[]{:S(2)}) copy-start(bf16[1,2048,384]{2,1,0:T(8,128)(2,1)} %param.11) | copy-start | bytes 4718596
  7.2 54.8 %all-gather.3.cloned.1.call-start = ((), (), s32[]{:S(2)}) async-start(), calls=%async_computation.7 | async-start | bytes 2785280 | tf_op jit(solution)/shard_map/all_gather | solution.py:23
  10.8 139.0 %all-gather.5.cloned.1.call-start = ((), (), s32[]{:S(2)}) async-start(), calls=%async_computation.8 | async-start | bytes 14155776 | tf_op jit(solution)/shard_map/all_gather | solution.py:60
  67.1 1.6 slice-start
  130.3 24.3 %copy-start.6 = (bf16[1,2048,384]{2,1,0:T(8,128)(2,1)S(1)}, bf16[1,2048,384]{2,1,0:T(8,128)(2,1)}, u32[]{:S(2)}) copy-start(bf16[1,2048,384]{2,1,0:T(8,128)(2,1)} %param.12) | copy-start | bytes 4718596
  149.8 5.1 %copy-start.8 = (bf16[2,1152,2048]{2,1,0:T(8,128)(2,1)S(1)}, bf16[2,1152,2048]{2,1,0:T(8,128)(2,1)}, u32[]{:S(2)}) copy-start(bf16[2,1152,2048]{2,1,0:T(8,128)(2,1)} %all-gather.5.cloned.1.call-done) | copy-start | bytes 28311556
  154.9 2.4 copy-start.4
  154.9 2.4 copy-start.9
  157.4 3.9 %copy-start.5 = (f32[1152,384]{0,1:T(8,128)}, f32[1152,384]{0,1:T(8,128)S(1)}, u32[]{:S(2)}) copy-start(f32[1152,384]{0,1:T(8,128)S(1)} %fusion.9) | copy-start | bytes 5308420
  164.4 8.6 %all-to-all-start.3 = ((bf16[4,4,72]{2,0,1:T(4,128)(2,1)}), bf16[4,4,72]{2,0,1:T(4,128)(2,1)S(1)}, u32[]{:S(2)}, u32[]{:S(2)}) async-start(bf16[4,4,72]{2,0,1:T(4,128)(2,1)} %copy.36), calls=%async_computation.5 | async-start | bytes 8192 | tf_op jit(solution)/shard_map/all_to_all | solution.py:106
  168.3 50.2 %reduce-scatter.4.cloned.1.call-start = ((), (), s32[]{:S(2)}) async-start(), calls=%async_computation.9 | async-start | bytes 14155776 | tf_op jit(solution)/shard_map/reduce_scatter | solution.py:97
  193.6 2.7 copy-start.2
  193.6 2.7 copy-start.7
  222.9 32.1 %all-to-all-start.2 = ((bf16[4,4,72,1024]{3,2,0,1:T(8,128)(2,1)}), bf16[4,4,72,1024]{3,2,0,1:T(8,128)(2,1)S(1)}, u32[]{:S(2)}, u32[]{:S(2)}) async-start(bf16[4,4,72,1024]{3,2,0,1:T(8,128)(2,1)} %copy.34), calls=%async_computation.3 | async-start | bytes 4718592 | tf_op jit(solution)/shard_map/all_to_all | solution.py:103
  226.8 47.9 %reduce-scatter.8.cloned.1.call-start = ((), (), s32[]{:S(2)}) async-start(), calls=%async_computation.11 | async-start | bytes 20480 | tf_op jit(solution)/shard_map/reduce_scatter | solution.py:119
  227.4 74.1 %reduce-scatter.6.cloned.1.call-start = ((), (), s32[]{:S(2)}) async-start(), calls=%async_computation.10 | async-start | bytes 2621440 | tf_op jit(solution)/shard_map/reduce_scatter | solution.py:113
  257.3 1.2 copy-start.10
  258.4 12.3 %slice-start.1 = ((s8[9437184]{0:T(1024)(128)(4,1)}), s8[4194304]{0:T(1024)(128)(4,1)S(1)}, s32[]{:S(2)}) async-start(s8[9437184]{0:T(1024)(128)(4,1)} %bitcast.89), calls=%async_computation.13 | async-start | bytes 8388608
  258.4 12.3 %slice-start.2 = ((s8[9437184]{0:T(1024)(128)(4,1)}), s8[4194304]{0:T(1024)(128)(4,1)S(1)}, s32[]{:S(2)}) async-start(s8[9437184]{0:T(1024)(128)(4,1)} %bitcast.89), calls=%async_computation.14 | async-start | bytes 8388608
  264.3 6.4 %copy-start.3 = (bf16[1152,384]{0,1:T(8,128)(2,1)S(1)}, bf16[1152,384]{0,1:T(8,128)(2,1)}, u32[]{:S(2)}) copy-start(bf16[1152,384]{0,1:T(8,128)(2,1)} %copy-done.2) | copy-start | bytes 2654212
  264.3 6.4 %slice-start.3 = ((s8[9437184]{0:T(1024)(128)(4,1)}), s8[1048576]{0:T(1024)(128)(4,1)S(1)}, s32[]{:S(2)}) async-start(s8[9437184]{0:T(1024)(128)(4,1)} %bitcast.89), calls=%async_computation.15 | async-start | bytes 2097152
  270.7 32.5 %copy-start.1 = (bf16[1,2048,384]{2,1,0:T(8,128)(2,1)S(1)}, bf16[1,2048,384]{2,1,0:T(8,128)(2,1)}, u32[]{:S(2)}) copy-start(bf16[1,2048,384]{2,1,0:T(8,128)(2,1)} %param.11) | copy-start | bytes 4718596
Sparse Core Ops, SparseCore 0:
  10.9 51.0 all-gather.2
  130.5 19.3 all-gather.4
  201.6 16.8 reduce-scatter.3
  230.2 20.4 reduce-scatter.7
  257.4 44.0 reduce-scatter.5
